TPU v7x, 32 devices: a whole 2x2x4 slice. The times are simulated.
32 devices in a mesh: dom: 8 (over z, y), rep: 4 (over x, core).
Axes of the slice: x: 2, y: 2, z: 4, core: 2. Of those that a mesh axis runs over, the one named last changes fastest.
Arguments:
- rhs: float32 [256, 32, 128], P(('dom', 'rep')), may hold values from -15 to 15
- precond: float32 [256, 128], P(('dom', 'rep')), may hold values from 0.25 to 1
- diag_tiles: bfloat16 [256, 128, 128], P(('dom', 'rep')), may hold values from -0.08 to 6.08
- off_tiles: bfloat16 [256, 2, 128, 128], P(('dom', 'rep')), may hold values from -0.119628906 to 0.119628906
- off_cols: int32 [256, 2], P(('dom', 'rep')), may hold values from 0 to 7
- link_tiles: bfloat16 [32, 128, 128], P(('dom', 'rep')), may hold values from -0.19921875 to 0.19921875
- contact_tiles: bfloat16 [512, 128, 128], P(('dom', 'rep')), may hold values from -0.29882812 to 0.29882812
- contact_owner: int32 [512, 1], P(('dom', 'rep')), may hold values from 0 to 3; in each aligned block of 16 rows (0 to 15, 16 to 31, ...) at most 8 rows name the same one
- contact_anode: int32 [512], P(('dom', 'rep')), may hold values from 0 to 7
- contact_bnode: int32 [512], P(('dom', 'rep')), may hold values from 0 to 7
Outputs:
- solution: float32 [256, 32, 128], P(('dom', 'rep'))
- residual: float32 [256, 32, 128], P(('dom', 'rep'))
Inputs may be any that keep to these rules, and one draw needn't show every extreme that they name: `contact_owner`: among the rows of one device no rep index is named by more than 8 rows.
All inputs are finite; a program needn't handle non-finite values.
Results may differ from a plain program's by a relative error of at most 0.03.
Values may be sent and summed in bfloat16 or wider, within the bound.
No kernel may reach another device: no remote copies, remote signals or barrier semaphores. Data moves between devices by JAX's collectives and lax.ppermute only.
A program may use at most 64 MiB of HBM per device.

v0:
```python
import jax
import jax.numpy as jnp
from jax import lax
from jax.sharding import PartitionSpec as P

B = 128
ITERS = 4
CAP = 8


def from_behind(value, axis, steps):
    count = lax.axis_size(axis)
    pairs = [(source, (source + steps) % count) for source in range(count)]
    return lax.ppermute(value, axis, pairs)


def partner(value, axis, distance):
    return lax.ppermute(value, axis, [(i, i ^ 1 << distance) for i in range(lax.axis_size(axis))])


def local_stiffness(rounded, diag_tiles, off_tiles, off_cols):
    nodes = rounded.shape[0]
    result = jnp.einsum("nrk,nkj->nrj", rounded, diag_tiles, preferred_element_type=jnp.float32)
    picked = rounded[off_cols]
    result = result + jnp.einsum(
        "nmrk,nmkj->nrj", picked, off_tiles, preferred_element_type=jnp.float32
    )
    mirror = jnp.einsum("nrk,nmjk->nmrj", rounded, off_tiles, preferred_element_type=jnp.float32)
    flat_cols = off_cols.reshape(-1)
    onehot = (flat_cols[:, None] == jnp.arange(nodes, dtype=jnp.int32)[None, :]).astype(jnp.float32)
    mirror = mirror.reshape(flat_cols.shape[0], rounded.shape[1], rounded.shape[2])
    return result + jnp.einsum("pn,prj->nrj", onehot, mirror, precision=lax.Precision.HIGHEST)


def contact_pairs(vector, other, near_index, far_index, contact_set):
    difference = (vector[near_index] - other[far_index]).astype(jnp.bfloat16)
    multiplier = jnp.einsum(
        "srk,skj->srj", difference, contact_set, preferred_element_type=jnp.float32
    ).astype(jnp.bfloat16)
    return jnp.einsum("srj,skj->srk", multiplier, contact_set, preferred_element_type=jnp.float32)


def collect(values, index, nodes):
    onehot = (index[:, None] == jnp.arange(nodes, dtype=jnp.int32)[None, :]).astype(jnp.float32)
    return jnp.einsum("sn,srk->nrk", onehot, values, precision=lax.Precision.HIGHEST)


def apply_operator(
    vector, diag_tiles, off_tiles, off_cols, link_tile, contact_set, near_index, far_index
):
    nodes = vector.shape[0]
    rounded = vector.astype(jnp.bfloat16)
    result = local_stiffness(rounded, diag_tiles, off_tiles, off_cols)
    before = from_behind(rounded[nodes - 1], "rep", 1)
    first_add = jnp.dot(before, link_tile, preferred_element_type=jnp.float32)
    back_term = lax.dot_general(
        rounded[0], link_tile, (((1,), (1,)), ((), ())), preferred_element_type=jnp.float32
    )
    after = from_behind(back_term, "rep", -1)
    result = result.at[0].add(first_add)
    result = result.at[nodes - 1].add(after)
    other = partner(vector.astype(jnp.bfloat16), "dom", 0).astype(vector.dtype)
    terms = contact_pairs(vector, other, near_index, far_index, contact_set)
    result = result + collect(terms, near_index, nodes)
    far_terms = partner(collect(terms, far_index, nodes).astype(jnp.bfloat16), "dom", 0).astype(
        jnp.float32
    )
    result = result - far_terms
    return result


def body(
    rhs,
    precond,
    diag_tiles,
    off_tiles,
    off_cols,
    link_tiles,
    contact_tiles,
    contact_owner,
    contact_anode,
    contact_bnode,
):
    groups = lax.axis_size("rep")
    target = contact_owner[:, 0]
    choose = (target[:, None] == jnp.arange(groups, dtype=jnp.int32)[None, :]).astype(jnp.int32)
    rank = jnp.sum((jnp.cumsum(choose, axis=0) - choose) * choose, axis=1)
    send_set = jnp.zeros((groups, CAP, B, B), jnp.bfloat16).at[target, rank].set(contact_tiles)
    labels = jnp.stack([contact_anode, contact_bnode], axis=1)
    send_labels = jnp.zeros((groups, CAP, 2), jnp.int32).at[target, rank].set(labels)
    got_set, got_labels = (
        lax.all_to_all(send_set, "rep", split_axis=0, concat_axis=0, tiled=True),
        lax.all_to_all(send_labels, "rep", split_axis=0, concat_axis=0, tiled=True),
    )
    slots = groups * CAP
    contact_set = got_set.reshape(slots, B, B)
    got_labels = got_labels.reshape(slots, 2)
    near_index = got_labels[:, 0]
    far_index = got_labels[:, 1]
    link_tile = link_tiles[0]
    scale = precond[:, None, :]
    solution = jnp.zeros_like(rhs)
    residual = rhs
    preconditioned = scale * residual
    direction = preconditioned
    res_dot = lax.psum(jnp.sum(residual * preconditioned, axis=(0, 2)), ("dom", "rep"))
    for step in range(ITERS):
        image = apply_operator(
            direction,
            diag_tiles,
            off_tiles,
            off_cols,
            link_tile,
            contact_set,
            near_index,
            far_index,
        )
        curve = lax.psum(jnp.sum(direction * image, axis=(0, 2)), ("dom", "rep"))
        alpha = res_dot / curve
        solution = solution + alpha[None, :, None] * direction
        residual = residual - alpha[None, :, None] * image
        preconditioned = scale * residual
        next_dot = lax.psum(jnp.sum(residual * preconditioned, axis=(0, 2)), ("dom", "rep"))
        direction = preconditioned + (next_dot / res_dot)[None, :, None] * direction
        res_dot = next_dot
    return (solution, residual)


def solution(mesh):
    in_specs = (
        P(("dom", "rep"), None, None),
        P(("dom", "rep"), None),
        P(("dom", "rep"), None, None),
        P(("dom", "rep"), None, None, None),
        P(("dom", "rep"), None),
        P(("dom", "rep"), None, None),
        P(("dom", "rep"), None, None),
        P(("dom", "rep"), None),
        P(("dom", "rep")),
        P(("dom", "rep")),
    )
    out_specs = (P(("dom", "rep"), None, None), P(("dom", "rep"), None, None))
    return jax.shard_map(body, mesh=mesh, in_specs=in_specs, out_specs=out_specs, check_vma=False)
```

profile of v0, /device:TPU:0, one launch (start us, length us, event | category | flops | bytes accessed | tf_op | source)
XLA Modules:
  0.0 372.2 jit_solution(10462506235294913822)
XLA Ops:
  0.7 0.7 copy-done.13
  1.7 0.7 pad_add_fusion
  2.4 1.3 scatter_fusion
  3.8 0.7 copy.71
  4.4 4.2 %all-to-all-start = ((s32[4,8,2]{1,2,0:T(2,128)}), s32[4,8,2]{1,2,0:T(2,128)S(1)}, u32[]{:S(2)}, u32[]{:S(2)}) async-start(s32[4,8,2]{1,2,0:T(2,128)} %copy.71), calls=%async_computation | async-start | bytes 8192 | tf_op jit(solution)/shard_map/all_to_all | solution.py:93
  8.7 2.1 collective-permute-start.2
  11.1 1.6 collective-permute-start.1
  13.1 0.6 gather_fusion
  13.7 0.3 fusion.57
  14.1 0.4 fusion.42
  14.7 1.2 broadcast_in_dim.8
  15.9 2.8 scatter_fusion.1
  18.7 3.5 all-to-all-start.1
  22.3 0.6 gather_fusion.1
  23.1 1.4 gather_fusion.2
  24.5 12.1 %all-to-all-done.1 = bf16[4,8,128,128]{3,2,1,0:T(8,128)(2,1)S(1)} async-done(((bf16[4,8,128,128]{3,2,1,0:T(8,128)(2,1)}), bf16[4,8,128,128]{3,2,1,0:T(8,128)(2,1)S(1)}, u32[]{:S(2)}, u32[]{:S(2)}) %all-to-all-start.1) | async-done | bytes 1048608 | tf_op jit(solution)/shard_map/all_to_all | solution.py:92
  36.6 2.0 fusion
  38.6 0.6 fusion.32
  39.2 0.7 collective-permute-start.3
  39.9 0.6 fusion.34
  40.5 3.1 collective-permute-done.3
  43.7 39.5 %all-reduce = (f32[32]{0:T(128)S(1)}, f32[32]{0:T(128)S(1)}) all-reduce(f32[32]{0:T(128)S(1)} %get-tuple-element.99, f32[32]{0:T(128)S(1)} %get-tuple-element.98), channel_id=1, replica_groups=mesh['dom'=8,'rep'=4] {'dom','rep'}, use_global_device_ids=true, to_apply=%region_1.2 | all-reduce | flops 64 | bytes 512 | tf_op jit(solution)/shard_map/psum | solution.py:106
  83.4 40.3 %psum.58 = f32[32]{0:T(128)S(1)} all-reduce(f32[32]{0:T(128)S(1)} %get-tuple-element.112), channel_id=1, replica_groups=mesh['dom'=8,'rep'=4] {'dom','rep'}, use_global_device_ids=true, to_apply=%region_9.10 | all-reduce | flops 32 | bytes 256 | tf_op jit(solution)/shard_map/psum | solution.py:123
  123.9 2.3 collective-permute-start.6
  126.4 1.2 gather_fusion.3
  127.6 0.3 fusion.55
  128.0 0.6 gather_fusion.4
  128.6 0.4 fusion.40
  129.1 1.7 collective-permute-start.5
  131.0 1.1 collective-permute-done.4
  132.3 1.4 gather_fusion.5
  133.7 2.0 fusion.1
  135.6 0.6 fusion.28
  136.3 0.6 fusion.30
  136.9 4.0 %collective-permute-done.7 = bf16[8,32,128]{2,1,0:T(8,128)(2,1)S(1)} collective-permute-done((bf16[8,32,128]{2,1,0:T(8,128)(2,1)S(1)}, bf16[8,32,128]{2,1,0:T(8,128)(2,1)S(1)}, u32[]{:S(2)}, u32[]{:S(2)}) %collective-permute-start.7) | collective-permute-done | bytes 65568 | tf_op jit(solution)/shard_map/ppermute | solution.py:18
  141.1 38.3 %psum.59 = f32[32]{0:T(128)S(1)} all-reduce(f32[32]{0:T(128)S(1)} %multiply_reduce_fusion.2), channel_id=1, replica_groups=mesh['dom'=8,'rep'=4] {'dom','rep'}, use_global_device_ids=true, to_apply=%region_11.12 | all-reduce | flops 32 | bytes 256 | tf_op jit(solution)/shard_map/psum | solution.py:118
  179.5 41.1 %psum.60 = f32[32]{0:T(128)S(1)} all-reduce(f32[32]{0:T(128)S(1)} %get-tuple-element.108), channel_id=1, replica_groups=mesh['dom'=8,'rep'=4] {'dom','rep'}, use_global_device_ids=true, to_apply=%region_13.14 | all-reduce | flops 32 | bytes 256 | tf_op jit(solution)/shard_map/psum | solution.py:123
  220.7 2.3 collective-permute-start.10
  223.2 1.2 gather_fusion.6
  224.8 0.6 gather_fusion.7
  225.5 0.4 fusion.38
  226.1 1.7 collective-permute-start.9
  228.0 1.1 collective-permute-done.8
  229.3 1.4 gather_fusion.8
  230.7 2.0 fusion.2
  232.7 0.6 fusion.24
  233.4 0.6 fusion.26
  234.0 3.9 %collective-permute-done.11 = bf16[8,32,128]{2,1,0:T(8,128)(2,1)S(1)} collective-permute-done((bf16[8,32,128]{2,1,0:T(8,128)(2,1)S(1)}, bf16[8,32,128]{2,1,0:T(8,128)(2,1)S(1)}, u32[]{:S(2)}, u32[]{:S(2)}) %collective-permute-start.11) | collective-permute-done | bytes 65568 | tf_op jit(solution)/shard_map/ppermute | solution.py:18
  238.0 38.3 %psum.61 = f32[32]{0:T(128)S(1)} all-reduce(f32[32]{0:T(128)S(1)} %multiply_reduce_fusion.1), channel_id=1, replica_groups=mesh['dom'=8,'rep'=4] {'dom','rep'}, use_global_device_ids=true, to_apply=%region_15.16 | all-reduce | flops 32 | bytes 256 | tf_op jit(solution)/shard_map/psum | solution.py:118
  276.6 39.8 %psum.62 = f32[32]{0:T(128)S(1)} all-reduce(f32[32]{0:T(128)S(1)} %get-tuple-element.104), channel_id=1, replica_groups=mesh['dom'=8,'rep'=4] {'dom','rep'}, use_global_device_ids=true, to_apply=%region_17.18 | all-reduce | flops 32 | bytes 256 | tf_op jit(solution)/shard_map/psum | solution.py:123
  316.5 2.3 collective-permute-start.14
  319.0 0.6 gather_fusion.9
  319.6 0.3 fusion.51
  320.0 0.6 gather_fusion.10
  320.6 0.4 fusion.36
  321.1 1.7 collective-permute-start.13
  323.0 1.1 collective-permute-done.12
  324.3 1.4 gather_fusion.11
  325.7 2.0 fusion.3
  327.6 0.6 fusion.20
  328.3 0.6 fusion.22
  328.9 3.7 collective-permute-done.15
  332.7 38.6 %psum.63 = f32[32]{0:T(128)S(1)} all-reduce(f32[32]{0:T(128)S(1)} %multiply_reduce_fusion), channel_id=1, replica_groups=mesh['dom'=8,'rep'=4] {'dom','rep'}, use_global_device_ids=true, to_apply=%region_19.20 | all-reduce | flops 32 | bytes 256 | tf_op jit(solution)/shard_map/psum | solution.py:118
  371.4 0.8 multiply_subtract_fusion
  (111 shorter events, 6.2 us)
Async XLA Ops:
  0.6 13.1 %copy-start = (bf16[8,2,128,128]{3,2,1,0:T(8,128)(2,1)S(1)}, bf16[8,2,128,128]{3,2,1,0:T(8,128)(2,1)}, u32[]{:S(2)}) copy-start(bf16[8,2,128,128]{3,2,1,0:T(8,128)(2,1)} %param.29) | copy-start | bytes 1572868
  0.6 0.7 copy-start.13
  0.7 8.0 %copy-start.2 = (f32[8,32,128]{2,1,0:T(8,128)S(1)}, f32[8,32,128]{2,1,0:T(8,128)}, u32[]{:S(2)}) copy-start(f32[8,32,128]{2,1,0:T(8,128)} %param.26) | copy-start | bytes 393220
  2.4 6.2 %copy-start.11 = (f32[8,128]{1,0:T(8,128)S(1)}, f32[8,128]{1,0:T(8,128)}, u32[]{:S(2)}) copy-start(f32[8,128]{1,0:T(8,128)} %param.27) | copy-start | bytes 12292
  2.4 10.4 %copy-start.1 = (bf16[8,128,128]{2,1,0:T(8,128)(2,1)S(1)}, bf16[8,128,128]{2,1,0:T(8,128)(2,1)}, u32[]{:S(2)}) copy-start(bf16[8,128,128]{2,1,0:T(8,128)(2,1)} %param.28) | copy-start | bytes 786436
  4.4 14.2 %all-to-all-start = ((s32[4,8,2]{1,2,0:T(2,128)}), s32[4,8,2]{1,2,0:T(2,128)S(1)}, u32[]{:S(2)}, u32[]{:S(2)}) async-start(s32[4,8,2]{1,2,0:T(2,128)} %copy.71), calls=%async_computation | async-start | bytes 8192 | tf_op jit(solution)/shard_map/all_to_all | solution.py:93
  8.7 2.3 copy-start.3
  8.7 14.4 %collective-permute-start.2 = (bf16[8,32,128]{2,1,0:T(8,128)(2,1)S(1)}, bf16[8,32,128]{2,1,0:T(8,128)(2,1)S(1)}, u32[]{:S(2)}, u32[]{:S(2)}) collective-permute-start(bf16[8,32,128]{2,1,0:T(8,128)(2,1)S(1)} %get-tuple-element.114), channel_id=1, source_target_pairs={{0,4},{4,0},{8,12},{12,8},{16,20},{20,16},{24,28},{28,24},{1,5},{5... | collective-permute-start | bytes 196616 | tf_op jit(solution)/shard_map/ppermute | solution.py:18
  10.8 1.9 copy-start.12
  10.8 12.1 %collective-permute-start = (bf16[32,128]{1,0:T(8,128)(2,1)S(1)}, bf16[32,128]{1,0:T(8,128)(2,1)S(1)}, u32[]{:S(2)}, u32[]{:S(2)}) collective-permute-start(bf16[32,128]{1,0:T(8,128)(2,1)S(1)} %slice_bitcast_fusion.11), channel_id=1, source_target_pairs={{0,1},{1,2},{2,3},{3,0},{4,5},{5,6},{6,7},{7,4},{8,9},{9,10},{10,1... | collective-permute-start | bytes 24584 | tf_op jit(solution)/shard_map/ppermute | solution.py:14
  11.1 12.0 %collective-permute-start.1 = (f32[32,128]{1,0:T(8,128)S(1)}, f32[32,128]{1,0:T(8,128)S(1)}, u32[]{:S(2)}, u32[]{:S(2)}) collective-permute-start(f32[32,128]{1,0:T(8,128)S(1)} %fusion.68), channel_id=1, source_target_pairs={{0,3},{1,0},{2,1},{3,2},{4,7},{5,4},{6,5},{7,6},{8,11},{9,8},{10,9... | collective-permute-start | bytes 49160 | tf_op jit(solution)/shard_map/ppermute | solution.py:14
  14.7 1.2 copy-start.8
  18.7 18.0 %all-to-all-start.1 = ((bf16[4,8,128,128]{3,2,1,0:T(8,128)(2,1)}), bf16[4,8,128,128]{3,2,1,0:T(8,128)(2,1)S(1)}, u32[]{:S(2)}, u32[]{:S(2)}) async-start(bf16[4,8,128,128]{3,2,1,0:T(8,128)(2,1)} %scatter_fusion.1), calls=%async_computation.1 | async-start | bytes 2097152 | tf_op jit(solution)/shard_map/all_to_all | solution.py:92
  39.2 4.3 %collective-permute-start.3 = (bf16[8,32,128]{2,1,0:T(8,128)(2,1)S(1)}, bf16[8,32,128]{2,1,0:T(8,128)(2,1)S(1)}, u32[]{:S(2)}, u32[]{:S(2)}) collective-permute-start(bf16[8,32,128]{2,1,0:T(8,128)(2,1)S(1)} %copy.166), channel_id=1, source_target_pairs={{0,4},{4,0},{8,12},{12,8},{16,20},{20,16},{24,28},{28,24},{1,5},{5... | collective-permute-start | bytes 196616 | tf_op jit(solution)/shard_map/ppermute | solution.py:18
  123.9 8.4 %collective-permute-start.6 = (bf16[8,32,128]{2,1,0:T(8,128)(2,1)S(1)}, bf16[8,32,128]{2,1,0:T(8,128)(2,1)S(1)}, u32[]{:S(2)}, u32[]{:S(2)}) collective-permute-start(bf16[8,32,128]{2,1,0:T(8,128)(2,1)S(1)} %get-tuple-element.110), channel_id=1, source_target_pairs={{0,4},{4,0},{8,12},{12,8},{16,20},{20,16},{24,28},{28,24},{1,5},{5... | collective-permute-start | bytes 196616 | tf_op jit(solution)/shard_map/ppermute | solution.py:18
  128.6 2.2 copy-start.9
  129.0 3.1 collective-permute-start.4
  129.1 3.2 collective-permute-start.5
  136.3 4.6 %collective-permute-start.7 = (bf16[8,32,128]{2,1,0:T(8,128)(2,1)S(1)}, bf16[8,32,128]{2,1,0:T(8,128)(2,1)S(1)}, u32[]{:S(2)}, u32[]{:S(2)}) collective-permute-start(bf16[8,32,128]{2,1,0:T(8,128)(2,1)S(1)} %copy.165), channel_id=1, source_target_pairs={{0,4},{4,0},{8,12},{12,8},{16,20},{20,16},{24,28},{28,24},{1,5},{5... | collective-permute-start | bytes 196616 | tf_op jit(solution)/shard_map/ppermute | solution.py:18
  179.5 41.2 %copy-start.6 = (f32[8,32,128]{2,1,0:T(8,128)}, f32[8,32,128]{2,1,0:T(8,128)S(1)}, u32[]{:S(2)}) copy-start(f32[8,32,128]{2,1,0:T(8,128)S(1)} %get-tuple-element.109) | copy-start | bytes 393220
  220.7 8.6 %collective-permute-start.10 = (bf16[8,32,128]{2,1,0:T(8,128)(2,1)S(1)}, bf16[8,32,128]{2,1,0:T(8,128)(2,1)S(1)}, u32[]{:S(2)}, u32[]{:S(2)}) collective-permute-start(bf16[8,32,128]{2,1,0:T(8,128)(2,1)S(1)} %get-tuple-element.106), channel_id=1, source_target_pairs={{0,4},{4,0},{8,12},{12,8},{16,20},{20,16},{24,28},{28,24},{1,5},{5... | collective-permute-start | bytes 196616 | tf_op jit(solution)/shard_map/ppermute | solution.py:18
  225.5 2.4 copy-start.10
  225.8 3.3 collective-permute-start.8
  226.1 3.2 collective-permute-start.9
  233.3 4.6 %collective-permute-start.11 = (bf16[8,32,128]{2,1,0:T(8,128)(2,1)S(1)}, bf16[8,32,128]{2,1,0:T(8,128)(2,1)S(1)}, u32[]{:S(2)}, u32[]{:S(2)}) collective-permute-start(bf16[8,32,128]{2,1,0:T(8,128)(2,1)S(1)} %copy.164), channel_id=1, source_target_pairs={{0,4},{4,0},{8,12},{12,8},{16,20},{20,16},{24,28},{28,24},{1,5},{5... | collective-permute-start | bytes 196616 | tf_op jit(solution)/shard_map/ppermute | solution.py:18
  233.9 42.4 %copy-start.7 = (f32[8,32,128]{2,1,0:T(8,128)S(1)}, f32[8,32,128]{2,1,0:T(8,128)}, u32[]{:S(2)}) copy-start(f32[8,32,128]{2,1,0:T(8,128)} %copy-done.6) | copy-start | bytes 393220
  276.6 39.9 %copy-start.4 = (f32[8,32,128]{2,1,0:T(8,128)}, f32[8,32,128]{2,1,0:T(8,128)S(1)}, u32[]{:S(2)}) copy-start(f32[8,32,128]{2,1,0:T(8,128)S(1)} %get-tuple-element.105) | copy-start | bytes 393220
  316.5 7.8 %collective-permute-start.14 = (bf16[8,32,128]{2,1,0:T(8,128)(2,1)S(1)}, bf16[8,32,128]{2,1,0:T(8,128)(2,1)S(1)}, u32[]{:S(2)}, u32[]{:S(2)}) collective-permute-start(bf16[8,32,128]{2,1,0:T(8,128)(2,1)S(1)} %get-tuple-element.102), channel_id=1, source_target_pairs={{0,4},{4,0},{8,12},{12,8},{16,20},{20,16},{24,28},{28,24},{1,5},{5... | collective-permute-start | bytes 196616 | tf_op jit(solution)/shard_map/ppermute | solution.py:18
  321.0 3.1 collective-permute-start.12
  321.1 3.2 collective-permute-start.13
  328.3 4.3 %collective-permute-start.15 = (bf16[8,32,128]{2,1,0:T(8,128)(2,1)S(1)}, bf16[8,32,128]{2,1,0:T(8,128)(2,1)S(1)}, u32[]{:S(2)}, u32[]{:S(2)}) collective-permute-start(bf16[8,32,128]{2,1,0:T(8,128)(2,1)S(1)} %copy.163), channel_id=1, source_target_pairs={{0,4},{4,0},{8,12},{12,8},{16,20},{20,16},{24,28},{28,24},{1,5},{5... | collective-permute-start | bytes 196616 | tf_op jit(solution)/shard_map/ppermute | solution.py:18
  328.9 42.5 %copy-start.5 = (f32[8,32,128]{2,1,0:T(8,128)S(1)}, f32[8,32,128]{2,1,0:T(8,128)}, u32[]{:S(2)}) copy-start(f32[8,32,128]{2,1,0:T(8,128)} %copy-done.4) | copy-start | bytes 393220
where the time goes:
time: 373 us; the launch traced here: 372 us
  blocking collectives  276 us (74%)
  waiting for transfers between devices  30.1 us (8%)
  starting transfers between devices  25.1 us (7%)
  local copies, waits for them, and re-layouts  18.9 us (5%)
  matrix products  17.6 us (5%)
    psum x4, blocking collectives, body(): lax.psum(jnp.sum(residual * preconditioned, axis=(0, 2)), ('dom', 'rep'))  161 us
    psum x3, blocking collectives, body(): curve = lax.psum(jnp.sum(direction * image, axis=(0, 2)), ('dom', 'rep'))  115 us
    ppermute x8, waiting for transfers between devices, partner(): lax.ppermute(value, axis, [(i, i ^ 1 << distance) for i in range(lax.axis...  14.6 us
    all_to_all x1, waiting for transfers between devices, body(): lax.all_to_all(send_set, 'rep', split_axis=0, concat_axis=0, tiled=True)  12.1 us
    ppermute x8, starting transfers between devices, partner(): lax.ppermute(value, axis, [(i, i ^ 1 << distance) for i in range(lax.axis...  10 us
    gather x8, local copies, waits for them, and re-layouts, contact_pairs(): difference = (vector[near_index] - other[far_index]).astype(jnp.bfloat16)  7.96 us
    dot_general x4, matrix products, contact_pairs(): jnp.einsum('srj,skj->srk', multiplier, contact_set, preferred_element_typ...  7.84 us
  transfers between devices with their start and end apart: 18, of which 8 were waited for; matrix products, arithmetic and copies ran while one was open for 5% of the time, Pallas kernels for 0%

commit v1 on v0

--- a/solution.py
+++ b/solution.py
@@ -120,7 +120,7 @@
         solution = solution + alpha[None, :, None] * direction
         residual = residual - alpha[None, :, None] * image
         preconditioned = scale * residual
-        next_dot = lax.psum(jnp.sum(residual * preconditioned, axis=(0, 2)), ("dom", "rep"))
+        next_dot = lax.psum(lax.psum(jnp.sum(residual * preconditioned, axis=(0, 2)), "rep"), "dom")
         direction = preconditioned + (next_dot / res_dot)[None, :, None] * direction
         res_dot = next_dot
     return (solution, residual)

time: 373 us -> 324 us (0.87)
  blocking collectives: 276 us -> 233 us
  waiting for transfers between devices: 30.1 us -> 24.5 us
    psum x4 -> x1, blocking collectives: 161 us -> 39.5 us  [body(): lax.psum(jnp.sum(residual * preconditioned, axis=(0, 2)), ('dom', 'rep'))]
    psum x0 -> x6, blocking collectives: none -> 80.4 us  [the longest x3 62.1 us: body(): lax.psum(lax.psum(jnp.sum(residual * preconditioned, axis=(0, 2)), 'rep')...]
    ppermute x8, waiting for transfers between devices: 14.6 us -> 9.05 us  [partner(): lax.ppermute(value, axis, [(i, i ^ 1 << distance) for i in range(lax.axis...]
  transfers between devices with their start and end apart: 18 -> 18, of which waited for: 8 -> 8; matrix products, arithmetic and copies ran while one was open for 5% -> 6% of each run, Pallas kernels for 0% -> 0%
where the time goes in v1:
time: 324 us; the launch traced here: 322 us
  blocking collectives  233 us (72%)
  waiting for transfers between devices  24.5 us (8%)
  starting transfers between devices  24.1 us (7%)
  local copies, waits for them, and re-layouts  18.9 us (6%)
  matrix products  17.6 us (5%)
  other arithmetic  3.45 us (1%)
    psum x3, blocking collectives, body(): curve = lax.psum(jnp.sum(direction * image, axis=(0, 2)), ('dom', 'rep'))  113 us
    psum x3, blocking collectives, body(): lax.psum(lax.psum(jnp.sum(residual * preconditioned, axis=(0, 2)), 'rep')...  62.1 us
    psum x1, blocking collectives, body(): lax.psum(jnp.sum(residual * preconditioned, axis=(0, 2)), ('dom', 'rep'))  39.5 us
    psum x3, blocking collectives, body(): lax.psum(jnp.sum(residual * preconditioned, axis=(0, 2)), 'rep')  18.3 us
    all_to_all x1, waiting for transfers between devices, body(): lax.all_to_all(send_set, 'rep', split_axis=0, concat_axis=0, tiled=True)  12.1 us
    ppermute x8, starting transfers between devices, partner(): lax.ppermute(value, axis, [(i, i ^ 1 << distance) for i in range(lax.axis...  9.24 us
    ppermute x8, waiting for transfers between devices, partner(): lax.ppermute(value, axis, [(i, i ^ 1 << distance) for i in range(lax.axis...  9.05 us
    gather x8, local copies, waits for them, and re-layouts, contact_pairs(): difference = (vector[near_index] - other[far_index]).astype(jnp.bfloat16)  7.96 us
  transfers between devices with their start and end apart: 18, of which 8 were waited for; matrix products, arithmetic and copies ran while one was open for 6% of the time, Pallas kernels for 0%

profile of v1, /device:TPU:0, one launch (start us, length us, event | category | flops | bytes accessed | tf_op | source)
XLA Modules:
  0.0 322.4 jit_solution(1336385359122607985)
XLA Ops:
  0.7 0.7 copy-done.13
  1.7 0.7 pad_add_fusion
  2.4 1.3 scatter_fusion
  3.8 0.7 copy.71
  4.4 4.2 %all-to-all-start = ((s32[4,8,2]{1,2,0:T(2,128)}), s32[4,8,2]{1,2,0:T(2,128)S(1)}, u32[]{:S(2)}, u32[]{:S(2)}) async-start(s32[4,8,2]{1,2,0:T(2,128)} %copy.71), calls=%async_computation | async-start | bytes 8192 | tf_op jit(solution)/shard_map/all_to_all | solution.py:93
  8.7 2.1 collective-permute-start.2
  11.1 1.6 collective-permute-start.1
  13.1 0.6 gather_fusion
  14.1 0.4 fusion.42
  14.7 1.2 broadcast_in_dim.8
  15.9 2.8 scatter_fusion.1
  18.7 3.5 %all-to-all-start.1 = ((bf16[4,8,128,128]{3,2,1,0:T(8,128)(2,1)}), bf16[4,8,128,128]{3,2,1,0:T(8,128)(2,1)S(1)}, u32[]{:S(2)}, u32[]{:S(2)}) async-start(bf16[4,8,128,128]{3,2,1,0:T(8,128)(2,1)} %scatter_fusion.1), calls=%async_computation.1 | async-start | bytes 2097152 | tf_op jit(solution)/shard_map/all_to_all | solution.py:92
  22.3 0.6 gather_fusion.1
  23.1 1.4 gather_fusion.2
  24.5 12.1 %all-to-all-done.1 = bf16[4,8,128,128]{3,2,1,0:T(8,128)(2,1)S(1)} async-done(((bf16[4,8,128,128]{3,2,1,0:T(8,128)(2,1)}), bf16[4,8,128,128]{3,2,1,0:T(8,128)(2,1)S(1)}, u32[]{:S(2)}, u32[]{:S(2)}) %all-to-all-start.1) | async-done | bytes 1048608 | tf_op jit(solution)/shard_map/all_to_all | solution.py:92
  36.6 2.0 fusion
  38.6 0.6 fusion.32
  39.2 0.7 collective-permute-start.3
  39.9 0.6 fusion.34
  40.5 3.1 collective-permute-done.3
  43.7 39.5 %all-reduce = (f32[32]{0:T(128)S(1)}, f32[32]{0:T(128)S(1)}) all-reduce(f32[32]{0:T(128)S(1)} %get-tuple-element.99, f32[32]{0:T(128)S(1)} %get-tuple-element.98), channel_id=1, replica_groups=mesh['dom'=8,'rep'=4] {'dom','rep'}, use_global_device_ids=true, to_apply=%region_1.2 | all-reduce | flops 64 | bytes 512 | tf_op jit(solution)/shard_map/psum | solution.py:106
  83.4 5.8 %psum.79 = f32[32]{0:T(128)S(1)} all-reduce(f32[32]{0:T(128)S(1)} %get-tuple-element.112), channel_id=1, replica_groups=mesh['dom'=8,'rep'=4] {'rep'}, use_global_device_ids=true, to_apply=%region_9.10 | all-reduce | flops 32 | bytes 256 | tf_op jit(solution)/shard_map/psum | solution.py:123
  89.3 20.9 %psum.80 = f32[32]{0:T(128)S(1)} all-reduce(f32[32]{0:T(128)S(1)} %psum.79), channel_id=1, replica_groups=mesh['dom'=8,'rep'=4] {'dom'}, use_global_device_ids=true, to_apply=%region_10.11 | all-reduce | flops 32 | bytes 256 | tf_op jit(solution)/shard_map/psum | solution.py:123
  110.5 1.2 gather_fusion.3
  112.2 0.6 gather_fusion.4
  112.8 0.4 fusion.40
  113.2 1.7 collective-permute-start.5
  115.2 1.1 collective-permute-done.4
  116.5 1.4 gather_fusion.5
  117.9 2.0 fusion.1
  119.8 0.6 fusion.28
  120.4 2.1 collective-permute-start.7
  122.5 0.6 fusion.30
  123.1 2.4 collective-permute-done.7
  125.6 37.1 %psum.81 = f32[32]{0:T(128)S(1)} all-reduce(f32[32]{0:T(128)S(1)} %multiply_reduce_fusion.2), channel_id=1, replica_groups=mesh['dom'=8,'rep'=4] {'dom','rep'}, use_global_device_ids=true, to_apply=%region_12.13 | all-reduce | flops 32 | bytes 256 | tf_op jit(solution)/shard_map/psum | solution.py:118
  163.0 6.6 %psum.82 = f32[32]{0:T(128)S(1)} all-reduce(f32[32]{0:T(128)S(1)} %get-tuple-element.108), channel_id=1, replica_groups=mesh['dom'=8,'rep'=4] {'rep'}, use_global_device_ids=true, to_apply=%region_14.15 | all-reduce | flops 32 | bytes 256 | tf_op jit(solution)/shard_map/psum | solution.py:123
  169.6 20.1 %psum.83 = f32[32]{0:T(128)S(1)} all-reduce(f32[32]{0:T(128)S(1)} %psum.82), channel_id=1, replica_groups=mesh['dom'=8,'rep'=4] {'dom'}, use_global_device_ids=true, to_apply=%region_15.16 | all-reduce | flops 32 | bytes 256 | tf_op jit(solution)/shard_map/psum | solution.py:123
  190.1 1.2 gather_fusion.6
  191.7 0.6 gather_fusion.7
  192.4 0.4 fusion.38
  192.8 1.8 collective-permute-start.9
  194.8 1.1 collective-permute-done.8
  196.0 1.4 gather_fusion.8
  197.4 2.0 fusion.2
  199.4 0.6 fusion.24
  200.0 2.1 collective-permute-start.11
  202.1 0.6 fusion.26
  202.7 1.7 collective-permute-done.11
  204.5 38.7 %psum.84 = f32[32]{0:T(128)S(1)} all-reduce(f32[32]{0:T(128)S(1)} %multiply_reduce_fusion.1), channel_id=1, replica_groups=mesh['dom'=8,'rep'=4] {'dom','rep'}, use_global_device_ids=true, to_apply=%region_17.18 | all-reduce | flops 32 | bytes 256 | tf_op jit(solution)/shard_map/psum | solution.py:118
  243.4 5.8 %psum.85 = f32[32]{0:T(128)S(1)} all-reduce(f32[32]{0:T(128)S(1)} %get-tuple-element.104), channel_id=1, replica_groups=mesh['dom'=8,'rep'=4] {'rep'}, use_global_device_ids=true, to_apply=%region_19.20 | all-reduce | flops 32 | bytes 256 | tf_op jit(solution)/shard_map/psum | solution.py:123
  249.2 21.0 %psum.86 = f32[32]{0:T(128)S(1)} all-reduce(f32[32]{0:T(128)S(1)} %psum.85), channel_id=1, replica_groups=mesh['dom'=8,'rep'=4] {'dom'}, use_global_device_ids=true, to_apply=%region_20.21 | all-reduce | flops 32 | bytes 256 | tf_op jit(solution)/shard_map/psum | solution.py:123
  270.6 0.6 gather_fusion.9
  271.6 0.6 gather_fusion.10
  272.3 0.4 fusion.36
  272.7 1.7 collective-permute-start.13
  274.6 1.1 collective-permute-done.12
  275.9 1.4 gather_fusion.11
  277.3 2.0 fusion.3
  279.3 0.6 fusion.20
  279.9 2.1 collective-permute-start.15
  282.0 0.6 fusion.22
  282.6 2.0 collective-permute-done.15
  284.7 36.9 %psum.87 = f32[32]{0:T(128)S(1)} all-reduce(f32[32]{0:T(128)S(1)} %multiply_reduce_fusion), channel_id=1, replica_groups=mesh['dom'=8,'rep'=4] {'dom','rep'}, use_global_device_ids=true, to_apply=%region_22.23 | all-reduce | flops 32 | bytes 256 | tf_op jit(solution)/shard_map/psum | solution.py:118
  321.6 0.8 multiply_subtract_fusion
  (114 shorter events, 6.8 us)
Async XLA Ops:
  0.6 13.1 %copy-start = (bf16[8,2,128,128]{3,2,1,0:T(8,128)(2,1)S(1)}, bf16[8,2,128,128]{3,2,1,0:T(8,128)(2,1)}, u32[]{:S(2)}) copy-start(bf16[8,2,128,128]{3,2,1,0:T(8,128)(2,1)} %param.29) | copy-start | bytes 1572868
  0.6 0.7 copy-start.13
  0.7 8.0 %copy-start.2 = (f32[8,32,128]{2,1,0:T(8,128)S(1)}, f32[8,32,128]{2,1,0:T(8,128)}, u32[]{:S(2)}) copy-start(f32[8,32,128]{2,1,0:T(8,128)} %param.26) | copy-start | bytes 393220
  2.4 6.2 %copy-start.11 = (f32[8,128]{1,0:T(8,128)S(1)}, f32[8,128]{1,0:T(8,128)}, u32[]{:S(2)}) copy-start(f32[8,128]{1,0:T(8,128)} %param.27) | copy-start | bytes 12292
  2.4 10.4 %copy-start.1 = (bf16[8,128,128]{2,1,0:T(8,128)(2,1)S(1)}, bf16[8,128,128]{2,1,0:T(8,128)(2,1)}, u32[]{:S(2)}) copy-start(bf16[8,128,128]{2,1,0:T(8,128)(2,1)} %param.28) | copy-start | bytes 786436
  4.4 14.2 %all-to-all-start = ((s32[4,8,2]{1,2,0:T(2,128)}), s32[4,8,2]{1,2,0:T(2,128)S(1)}, u32[]{:S(2)}, u32[]{:S(2)}) async-start(s32[4,8,2]{1,2,0:T(2,128)} %copy.71), calls=%async_computation | async-start | bytes 8192 | tf_op jit(solution)/shard_map/all_to_all | solution.py:93
  8.7 2.3 copy-start.3
  8.7 14.4 %collective-permute-start.2 = (bf16[8,32,128]{2,1,0:T(8,128)(2,1)S(1)}, bf16[8,32,128]{2,1,0:T(8,128)(2,1)S(1)}, u32[]{:S(2)}, u32[]{:S(2)}) collective-permute-start(bf16[8,32,128]{2,1,0:T(8,128)(2,1)S(1)} %get-tuple-element.114), channel_id=1, source_target_pairs={{0,4},{4,0},{8,12},{12,8},{16,20},{20,16},{24,28},{28,24},{1,5},{5... | collective-permute-start | bytes 196616 | tf_op jit(solution)/shard_map/ppermute | solution.py:18
  10.8 1.9 copy-start.12
  10.8 12.1 %collective-permute-start = (bf16[32,128]{1,0:T(8,128)(2,1)S(1)}, bf16[32,128]{1,0:T(8,128)(2,1)S(1)}, u32[]{:S(2)}, u32[]{:S(2)}) collective-permute-start(bf16[32,128]{1,0:T(8,128)(2,1)S(1)} %slice_bitcast_fusion.11), channel_id=1, source_target_pairs={{0,1},{1,2},{2,3},{3,0},{4,5},{5,6},{6,7},{7,4},{8,9},{9,10},{10,1... | collective-permute-start | bytes 24584 | tf_op jit(solution)/shard_map/ppermute | solution.py:14
  11.1 12.0 %collective-permute-start.1 = (f32[32,128]{1,0:T(8,128)S(1)}, f32[32,128]{1,0:T(8,128)S(1)}, u32[]{:S(2)}, u32[]{:S(2)}) collective-permute-start(f32[32,128]{1,0:T(8,128)S(1)} %fusion.68), channel_id=1, source_target_pairs={{0,3},{1,0},{2,1},{3,2},{4,7},{5,4},{6,5},{7,6},{8,11},{9,8},{10,9... | collective-permute-start | bytes 49160 | tf_op jit(solution)/shard_map/ppermute | solution.py:14
  14.7 1.2 copy-start.8
  18.7 18.0 %all-to-all-start.1 = ((bf16[4,8,128,128]{3,2,1,0:T(8,128)(2,1)}), bf16[4,8,128,128]{3,2,1,0:T(8,128)(2,1)S(1)}, u32[]{:S(2)}, u32[]{:S(2)}) async-start(bf16[4,8,128,128]{3,2,1,0:T(8,128)(2,1)} %scatter_fusion.1), calls=%async_computation.1 | async-start | bytes 2097152 | tf_op jit(solution)/shard_map/all_to_all | solution.py:92
  39.2 4.3 %collective-permute-start.3 = (bf16[8,32,128]{2,1,0:T(8,128)(2,1)S(1)}, bf16[8,32,128]{2,1,0:T(8,128)(2,1)S(1)}, u32[]{:S(2)}, u32[]{:S(2)}) collective-permute-start(bf16[8,32,128]{2,1,0:T(8,128)(2,1)S(1)} %copy.166), channel_id=1, source_target_pairs={{0,4},{4,0},{8,12},{12,8},{16,20},{20,16},{24,28},{28,24},{1,5},{5... | collective-permute-start | bytes 196616 | tf_op jit(solution)/shard_map/ppermute | solution.py:18
  110.3 6.2 %collective-permute-start.6 = (bf16[8,32,128]{2,1,0:T(8,128)(2,1)S(1)}, bf16[8,32,128]{2,1,0:T(8,128)(2,1)S(1)}, u32[]{:S(2)}, u32[]{:S(2)}) collective-permute-start(bf16[8,32,128]{2,1,0:T(8,128)(2,1)S(1)} %get-tuple-element.110), channel_id=1, source_target_pairs={{0,4},{4,0},{8,12},{12,8},{16,20},{20,16},{24,28},{28,24},{1,5},{5... | collective-permute-start | bytes 196616 | tf_op jit(solution)/shard_map/ppermute | solution.py:18
  112.8 2.2 copy-start.9
  113.2 3.1 collective-permute-start.4
  113.2 3.2 collective-permute-start.5
  120.4 5.0 %collective-permute-start.7 = (bf16[8,32,128]{2,1,0:T(8,128)(2,1)S(1)}, bf16[8,32,128]{2,1,0:T(8,128)(2,1)S(1)}, u32[]{:S(2)}, u32[]{:S(2)}) collective-permute-start(bf16[8,32,128]{2,1,0:T(8,128)(2,1)S(1)} %copy.165), channel_id=1, source_target_pairs={{0,4},{4,0},{8,12},{12,8},{16,20},{20,16},{24,28},{28,24},{1,5},{5... | collective-permute-start | bytes 196616 | tf_op jit(solution)/shard_map/ppermute | solution.py:18
  163.0 26.9 %copy-start.6 = (f32[8,32,128]{2,1,0:T(8,128)}, f32[8,32,128]{2,1,0:T(8,128)S(1)}, u32[]{:S(2)}) copy-start(f32[8,32,128]{2,1,0:T(8,128)S(1)} %get-tuple-element.109) | copy-start | bytes 393220
  189.8 6.2 %collective-permute-start.10 = (bf16[8,32,128]{2,1,0:T(8,128)(2,1)S(1)}, bf16[8,32,128]{2,1,0:T(8,128)(2,1)S(1)}, u32[]{:S(2)}, u32[]{:S(2)}) collective-permute-start(bf16[8,32,128]{2,1,0:T(8,128)(2,1)S(1)} %get-tuple-element.106), channel_id=1, source_target_pairs={{0,4},{4,0},{8,12},{12,8},{16,20},{20,16},{24,28},{28,24},{1,5},{5... | collective-permute-start | bytes 196616 | tf_op jit(solution)/shard_map/ppermute | solution.py:18
  192.3 2.2 copy-start.10
  192.7 3.1 collective-permute-start.8
  192.8 3.2 collective-permute-start.9
  200.0 4.3 %collective-permute-start.11 = (bf16[8,32,128]{2,1,0:T(8,128)(2,1)S(1)}, bf16[8,32,128]{2,1,0:T(8,128)(2,1)S(1)}, u32[]{:S(2)}, u32[]{:S(2)}) collective-permute-start(bf16[8,32,128]{2,1,0:T(8,128)(2,1)S(1)} %copy.164), channel_id=1, source_target_pairs={{0,4},{4,0},{8,12},{12,8},{16,20},{20,16},{24,28},{28,24},{1,5},{5... | collective-permute-start | bytes 196616 | tf_op jit(solution)/shard_map/ppermute | solution.py:18
  202.6 40.5 %copy-start.7 = (f32[8,32,128]{2,1,0:T(8,128)S(1)}, f32[8,32,128]{2,1,0:T(8,128)}, u32[]{:S(2)}) copy-start(f32[8,32,128]{2,1,0:T(8,128)} %copy-done.6) | copy-start | bytes 393220
  243.4 27.0 %copy-start.4 = (f32[8,32,128]{2,1,0:T(8,128)}, f32[8,32,128]{2,1,0:T(8,128)S(1)}, u32[]{:S(2)}) copy-start(f32[8,32,128]{2,1,0:T(8,128)S(1)} %get-tuple-element.105) | copy-start | bytes 393220
  270.4 5.5 %collective-permute-start.14 = (bf16[8,32,128]{2,1,0:T(8,128)(2,1)S(1)}, bf16[8,32,128]{2,1,0:T(8,128)(2,1)S(1)}, u32[]{:S(2)}, u32[]{:S(2)}) collective-permute-start(bf16[8,32,128]{2,1,0:T(8,128)(2,1)S(1)} %get-tuple-element.102), channel_id=1, source_target_pairs={{0,4},{4,0},{8,12},{12,8},{16,20},{20,16},{24,28},{28,24},{1,5},{5... | collective-permute-start | bytes 196616 | tf_op jit(solution)/shard_map/ppermute | solution.py:18
  272.6 3.1 collective-permute-start.12
  272.7 3.2 collective-permute-start.13
  279.9 4.6 %collective-permute-start.15 = (bf16[8,32,128]{2,1,0:T(8,128)(2,1)S(1)}, bf16[8,32,128]{2,1,0:T(8,128)(2,1)S(1)}, u32[]{:S(2)}, u32[]{:S(2)}) collective-permute-start(bf16[8,32,128]{2,1,0:T(8,128)(2,1)S(1)} %copy.163), channel_id=1, source_target_pairs={{0,4},{4,0},{8,12},{12,8},{16,20},{20,16},{24,28},{28,24},{1,5},{5... | collective-permute-start | bytes 196616 | tf_op jit(solution)/shard_map/ppermute | solution.py:18
  282.6 39.1 %copy-start.5 = (f32[8,32,128]{2,1,0:T(8,128)S(1)}, f32[8,32,128]{2,1,0:T(8,128)}, u32[]{:S(2)}) copy-start(f32[8,32,128]{2,1,0:T(8,128)} %copy-done.4) | copy-start | bytes 393220
